TPU v7x, 256 devices: a whole 4x4x8 slice. The times are simulated.
256 devices in a mesh: sample: 32 (over x, y, core), slab: 8 (over z).
Axes of the slice: x: 4, y: 4, z: 8, core: 2. Of those that a mesh axis runs over, the one named last changes fastest.
Arguments:
- volume: bfloat16 [4, 32, 32, 4096], P(None, 'sample', 'slab'), may hold values from -6 to 6
- cotangent: bfloat16 [128, 32, 8, 256], P(None, 'sample', 'slab'), may hold values from -0.5 to 0.5
- w_first: bfloat16 [27, 4, 32], replicated, may hold values from -0.625 to 0.625
- b_first: float32 [32], replicated, may hold values from -3 to 3
- w_second: bfloat16 [27, 32, 64], replicated, may hold values from -0.21875 to 0.21875
- b_second: float32 [64], replicated, may hold values from -3 to 3
- w_third: bfloat16 [27, 64, 128], replicated, may hold values from -0.15625 to 0.15625
- b_third: float32 [128], replicated, may hold values from -3 to 3
Outputs:
- features: bfloat16 [128, 32, 8, 256], P(None, 'sample', 'slab')
- kernel_grad_first: float32 [27, 4, 32], replicated
- bias_grad_first: float32 [32], replicated
- kernel_grad_second: float32 [27, 32, 64], replicated
- bias_grad_second: float32 [64], replicated
- kernel_grad_third: float32 [27, 64, 128], replicated
- bias_grad_third: float32 [128], replicated
All inputs are finite; a program needn't handle non-finite values.
Results may differ from a plain program's by a relative error of at most 0.02.
Values may be sent and summed in bfloat16 or wider, within the bound.
No kernel may reach another device: no remote copies, remote signals or barrier semaphores. Data moves between devices by JAX's collectives and lax.ppermute only.
A program may use at most 128 MiB of HBM per device.

v0:
```python
import jax
import jax.numpy as jnp
from jax import lax
from jax.sharding import PartitionSpec as P

SX = 32
CZ = 4


def with_halo(shard, sides, width):
    for axis, dim in sides:
        size, length = (lax.axis_size(axis), shard.shape[dim])
        up = [(i, (i + 1) % size) for i in range(size - 1)]
        down = [(j, i) for i, j in up]
        last = lax.slice_in_dim(shard, length - width, length, axis=dim)
        first = lax.slice_in_dim(shard, 0, width, axis=dim)
        before = lax.ppermute(last, axis, up)
        after = lax.ppermute(first, axis, down)
        shard = jnp.concatenate([before, shard, after], axis=dim)
    return shard


def silu_slope(values):
    sigmoid = jax.nn.sigmoid(values)
    return sigmoid * (1.0 + values * (1.0 - sigmoid))


def put_block(values, update, sample, depth_start):
    return lax.dynamic_update_slice(values, update, (0, sample, depth_start, 0))


def gather_taps(section, row_width):
    depth_len = section.shape[2] - 2
    plane_size = section.shape[3]
    flattened = jnp.pad(section, ((0, 0), (0, 0), (0, 0), (row_width + 1, row_width + 1)))
    column = lax.broadcasted_iota(jnp.int32, (1, 1, 1, plane_size), 3) % row_width
    left_mask = (column >= 1).astype(section.dtype)
    right_mask = (column <= row_width - 2).astype(section.dtype)
    pieces = []
    for tap_index in range(27):
        depth_start = tap_index // 9
        row_step = tap_index // 3 % 3 - 1
        col_step = tap_index % 3 - 1
        offset = row_width + 1 + row_step * row_width + col_step
        shifted = flattened[
            :, :, depth_start : depth_start + depth_len, offset : offset + plane_size
        ]
        if col_step < 0:
            shifted = shifted * left_mask
        elif col_step > 0:
            shifted = shifted * right_mask
        pieces.append(shifted)
    return jnp.concatenate(pieces, axis=0)


def apply_weight(patches, weight):
    flat_weight = weight.reshape(weight.shape[0] * weight.shape[1], weight.shape[2])
    return jnp.einsum("ko,kgzp->ogzp", flat_weight, patches, preferred_element_type=jnp.float32)


def weight_term(patches, grad_block, in_channels):
    summed = jnp.einsum("kgzp,ogzp->ko", patches, grad_block, preferred_element_type=jnp.float32)
    return summed.reshape(27, in_channels, grad_block.shape[0])


def pool_cells(values, row_width):
    channels, samples, depth_len, plane_size = values.shape
    row_count = plane_size // row_width
    grouped = values.reshape(
        channels, samples, depth_len // 2, 2, row_count // 2, 2, row_width // 2, 2
    )
    return grouped.mean(axis=(3, 5, 7)).reshape(channels, samples, depth_len // 2, plane_size // 4)


def spread_cells(values, coarse_width):
    channels, samples, depth_len, plane_size = values.shape
    row_count = plane_size // coarse_width
    grouped = values.reshape(channels, samples, depth_len, 1, row_count, 1, coarse_width, 1)
    grouped = jnp.broadcast_to(
        grouped, (channels, samples, depth_len, 2, row_count, 2, coarse_width, 2)
    )
    return grouped.reshape(channels, samples, 2 * depth_len, 4 * plane_size) * 0.125


def forward_layer(padded, weight, bias_values, row_width, depth_block, pooled_out):
    out_channels = weight.shape[2]
    samples, depth_total, plane_size = (padded.shape[1], padded.shape[2] - 2, padded.shape[3])
    per_sample = depth_total // depth_block
    pre_buffer = jnp.zeros((out_channels, samples, depth_total, plane_size), jnp.bfloat16)
    if pooled_out:
        out_buffer = jnp.zeros(
            (out_channels, samples, depth_total // 2, plane_size // 4), jnp.bfloat16
        )
    else:
        out_buffer = jnp.zeros_like(pre_buffer)

    def forward_block_step(block_index, buffers):
        sample = block_index // per_sample
        depth_start = block_index % per_sample * depth_block
        pre_values = (
            apply_weight(gather_taps(padded, row_width), weight) + bias_values[:, None, None, None]
        ).astype(jnp.bfloat16)
        activated = jax.nn.silu(pre_values.astype(jnp.float32))
        if pooled_out:
            result = put_block(
                buffers[1],
                pool_cells(activated, row_width).astype(jnp.bfloat16),
                sample,
                depth_start // 2,
            )
        else:
            result = put_block(buffers[1], activated.astype(jnp.bfloat16), sample, depth_start)
        return (put_block(buffers[0], pre_values, sample, depth_start), result)

    return lax.fori_loop(0, samples * per_sample, forward_block_step, (pre_buffer, out_buffer))


def weight_grads(padded, delta_values, row_width, depth_block, weight):
    samples, depth_total = (delta_values.shape[1], delta_values.shape[2])
    per_sample = depth_total // depth_block
    in_channels = weight.shape[1]

    def weight_block_step(block_index, summed):
        return summed + weight_term(gather_taps(padded, row_width), delta_values, in_channels)

    return lax.fori_loop(
        0, samples * per_sample, weight_block_step, jnp.zeros(weight.shape, jnp.float32)
    )


def data_grads(padded, flipped, row_width, depth_block):
    out_channels = flipped.shape[2]
    samples, depth_total, plane_size = (padded.shape[1], padded.shape[2] - 2, padded.shape[3])
    per_sample = depth_total // depth_block
    out_buffer = jnp.zeros((out_channels, samples, depth_total, plane_size), jnp.bfloat16)

    def data_block_step(block_index, buffer_now):
        sample = block_index // per_sample
        depth_start = block_index % per_sample * depth_block
        result = apply_weight(gather_taps(padded, row_width), flipped).astype(jnp.bfloat16)
        return put_block(buffer_now, result, sample, depth_start)

    return lax.fori_loop(0, samples * per_sample, data_block_step, out_buffer)


def bias_sum(delta_values):
    return jnp.sum(delta_values, axis=(1, 2, 3), dtype=jnp.float32)


def per_device(volume, cotangent, w_first, b_first, w_second, b_second, w_third, b_third):
    flipped_second = jnp.flip(w_second, 0).transpose(0, 2, 1)
    flipped_third = jnp.flip(w_third, 0).transpose(0, 2, 1)
    volume_padded = with_halo(volume, (("slab", 2),), 1)
    first_pre, first_pooled = forward_layer(volume_padded, w_first, b_first, SX, CZ, True)
    first_padded = with_halo(first_pooled, (("slab", 2),), 1)
    second_pre, second_pooled = forward_layer(
        first_padded, w_second, b_second, SX // 2, CZ // 2, True
    )
    coarse_depth = second_pooled.shape[2]
    third_padded = with_halo(second_pooled, (("slab", 2),), 1)
    third_pre, features = forward_layer(
        third_padded, w_third, b_third, SX // 4, coarse_depth, False
    )
    third_delta = (
        cotangent.astype(jnp.float32) * silu_slope(third_pre.astype(jnp.float32))
    ).astype(jnp.bfloat16)
    kernel_third = weight_grads(third_padded, third_delta, SX // 4, coarse_depth, w_third)
    bias_third = bias_sum(third_delta)
    kernel_third, bias_third = lax.psum((kernel_third, bias_third), ("sample", "slab"))
    delta_window = with_halo(third_delta, (("slab", 2),), 1)
    second_back = data_grads(delta_window, flipped_third, SX // 4, coarse_depth)
    second_delta = (
        spread_cells(second_back.astype(jnp.float32), SX // 4)
        * silu_slope(second_pre.astype(jnp.float32))
    ).astype(jnp.bfloat16)
    kernel_second = weight_grads(first_padded, second_delta, SX // 2, CZ // 2, w_second)
    bias_second = bias_sum(second_delta)
    delta_padded = with_halo(second_delta, (("slab", 2),), 1)
    first_back = data_grads(delta_padded, flipped_second, SX // 2, CZ // 2)
    first_delta = (
        spread_cells(first_back.astype(jnp.float32), SX // 2)
        * silu_slope(first_pre.astype(jnp.float32))
    ).astype(jnp.bfloat16)
    kernel_first = weight_grads(volume_padded, first_delta, SX, CZ, w_first)
    bias_first = bias_sum(first_delta)
    kernel_first, bias_first, kernel_second, bias_second = lax.psum(
        (kernel_first, bias_first, kernel_second, bias_second), ("sample", "slab")
    )
    return (
        features,
        kernel_first,
        bias_first,
        kernel_second,
        bias_second,
        kernel_third,
        bias_third,
    )


def solution(mesh):
    in_specs = (
        P(None, "sample", "slab", None),
        P(None, "sample", "slab", None),
        P(),
        P(),
        P(),
        P(),
        P(),
        P(),
    )
    out_specs = (P(None, "sample", "slab", None), P(), P(), P(), P(), P(), P())
    return jax.shard_map(
        per_device, mesh=mesh, in_specs=in_specs, out_specs=out_specs, check_vma=False
    )
```

profile of v0, /device:TPU:1, one launch (start us, length us, event | category | flops | bytes accessed | tf_op | source)
XLA Modules:
  0.0 395.6 jit_solution(9042423092520511804)
XLA Ops:
  7.2 1.0 copy.58
  8.3 4.4 %collective-permute-start = (bf16[4,1,1,4096]{3,0,2,1:T(4,128)(2,1)S(1)}, bf16[4,1,1,4096]{3,0,2,1:T(4,128)(2,1)S(1)}, u32[]{:S(2)}, u32[]{:S(2)}) collective-permute-start(bf16[4,1,1,4096]{3,0,2,1:T(4,128)(2,1)S(1)} %get-tuple-element.223), channel_id=1, source_target_pairs={{0,1},{1,2},{2,3},{3,4},{4,5},{5,6},{6,7},{8,9},{9,10},{10,11},{11... | collective-permute-start | bytes 98312 | tf_op jit(solution)/shard_map/ppermute | solution.py:17
  12.6 1.3 collective-permute-start.1
  14.0 0.6 fusion.115
  14.6 0.9 reverse_bitcast_fusion.1
  15.5 1.0 reverse_bitcast_fusion
  16.6 1.4 reshape.324
  18.0 0.6 copy-done.3
  18.6 0.6 copy-done.5
  19.4 1.3 slice_multiply_fusion.36
  20.7 1.7 slice_multiply_fusion.37
  22.4 16.2 %concatenate.62 = bf16[108,1,4,4096]{3,0,2,1:T(8,128)(2,1)} concatenate(bf16[4,1,4,4096]{3,0,2,1:T(4,128)(2,1)} %get-tuple-element.212, bf16[4,1,4,4096]{3,0,2,1:T(4,128)(2,1)S(1)} %get-tuple-element.218, bf16[4,1,4,4096]{3,0,2,1:T(4,128)(2,1)S(1)} %get-tuple-element.203, bf16[4,1,4,4096]{3,0,2,1:T(4,128)(2,1)} %get-tuple-element.211, ...), dimensions={0} | concatenate | bytes 7077888 | tf_op jit(solution)/shard_map/while/body/eval_jaxpr/concatenate | solution.py:53
  38.6 4.7 %fusion.10 = (f32[32,4,4096]{2,0,1:T(8,128)S(1)}, f32[32,4,4096]{2,0,1:T(8,128)}) fusion(f32[32]{0:T(128)} %param.11, bf16[108,32]{1,0:T(8,128)(2,1)} %reshape.324, bf16[108,1,4,4096]{3,0,2,1:T(8,128)(2,1)} %concatenate.62), kind=kOutput, calls=%fused_computation.14 | convolution fusion | flops 116916224 | bytes 7740288 | tf_op jit(solution)/shard_map/while/body/eval_jaxpr/ko,kgzp->ogzp/dot_general | solution.py:58
  43.2 4.6 %copy.65 = f32[32,4,4096]{0,2,1:T(8,128)} copy(f32[32,4,4096]{2,0,1:T(8,128)S(1)} %get-tuple-element.225) | data formatting | bytes 4194304 | tf_op jit(solution)/shard_map/while/body/eval_jaxpr/jit(silu)/mul | solution.py:103
  47.9 9.5 %reduce_sum.54 = f32[32,2,64,16]{0,3,2,1:T(8,128)S(1)} reduce(f32[32,2,2,64,2,16,2]{0,6,5,4,3,2,1:T(2,128)} %bitcast.123, f32[]{:T(128)} %constant.224.clone.1), dimensions={2,4,6}, to_apply=%region_0.1 | reduce | flops 458752 | bytes 2359300 | tf_op jit(solution)/shard_map/while/body/eval_jaxpr/reduce_sum | solution.py:72
  57.7 4.2 %collective-permute-start.2 = (bf16[32,1,1,1024]{3,0,2,1:T(8,128)(2,1)S(1)}, bf16[32,1,1,1024]{3,0,2,1:T(8,128)(2,1)S(1)}, u32[]{:S(2)}, u32[]{:S(2)}) collective-permute-start(bf16[32,1,1,1024]{3,0,2,1:T(8,128)(2,1)S(1)} %get-tuple-element.219), channel_id=1, source_target_pairs={{0,1},{1,2},{2,3},{3,4},{4,5},{5,6},{6,7},{8,9},{9,10},{10,11},{11... | collective-permute-start | bytes 196616 | tf_op jit(solution)/shard_map/ppermute | solution.py:17
  61.9 1.8 collective-permute-start.3
  63.7 3.3 collective-permute-done.3
  69.8 1.7 copy-done
  71.5 0.9 multiply_reduce_fusion
  72.6 0.4 reduce_sum.57
  73.1 1.3 collective-permute-start.5
  74.4 5.4 %collective-permute-start.4 = (bf16[64,1,1,256]{0,3,2,1:T(8,128)(2,1)S(1)}, bf16[64,1,1,256]{0,3,2,1:T(8,128)(2,1)S(1)}, u32[]{:S(2)}, u32[]{:S(2)}) collective-permute-start(bf16[64,1,1,256]{0,3,2,1:T(8,128)(2,1)S(1)} %fusion.106), channel_id=1, source_target_pairs={{0,1},{1,2},{2,3},{3,4},{4,5},{5,6},{6,7},{8,9},{9,10},{10,11},{11... | collective-permute-start | bytes 98312 | tf_op jit(solution)/shard_map/ppermute | solution.py:17
  79.8 0.7 copy.75
  80.9 6.6 %copy.74 = bf16[108,4096,4]{1,2,0:T(4,128)(2,1)} copy(bf16[108,4096,4]{1,0,2:T(8,128)(2,1)} %bitcast.125) | data formatting | bytes 7077888 | tf_op jit(solution)/shard_map/while/body/eval_jaxpr/kgzp,ogzp->ko/dot_general | solution.py:62
  87.6 0.8 slice_multiply_fusion.72
  88.5 3.4 concatenate.68
  91.8 0.6 copy.83
  92.5 1.4 convert_reduce_fusion.2
  93.9 1.3 collective-permute-start.7
  95.2 5.2 %collective-permute-start.6 = (bf16[128,1,1,256]{0,3,2,1:T(8,128)(2,1)S(1)}, bf16[128,1,1,256]{0,3,2,1:T(8,128)(2,1)S(1)}, u32[]{:S(2)}, u32[]{:S(2)}) collective-permute-start(bf16[128,1,1,256]{0,3,2,1:T(8,128)(2,1)S(1)} %get-tuple-element.156), channel_id=1, source_target_pairs={{0,1},{1,2},{2,3},{3,4},{4,5},{5,6},{6,7},{8,9},{9,10},{10,11},{11... | collective-permute-start | bytes 196616 | tf_op jit(solution)/shard_map/ppermute | solution.py:17
  100.4 1.3 fusion.107
  101.8 0.7 copy.85
  105.1 0.7 fusion.53
  106.6 4.6 %collective-permute-start.8 = (bf16[64,1,1,1024]{3,0,2,1:T(8,128)(2,1)S(1)}, bf16[64,1,1,1024]{3,0,2,1:T(8,128)(2,1)S(1)}, u32[]{:S(2)}, u32[]{:S(2)}) collective-permute-start(bf16[64,1,1,1024]{3,0,2,1:T(8,128)(2,1)S(1)} %get-tuple-element.165), channel_id=1, source_target_pairs={{0,1},{1,2},{2,3},{3,4},{4,5},{5,6},{6,7},{8,9},{9,10},{10,11},{11... | collective-permute-start | bytes 393224 | tf_op jit(solution)/shard_map/ppermute | solution.py:17
  111.1 1.5 collective-permute-start.9
  112.6 3.8 convolution_bitcast_fusion
  116.5 1.6 collective-permute-done.9
  121.8 1.3 fusion.35
  123.5 7.5 %broadcast_in_dim.14 = f32[32,2,2,64,2,16,2]{0,6,5,4,3,2,1:T(2,128)} broadcast(f32[32,2,64,16]{0,3,2,1:T(8,128)S(1)} %bitcast.130), dimensions={0,1,3,5} | broadcast | bytes 2359296 | tf_op jit(solution)/shard_map/broadcast_in_dim | solution.py:79
  131.0 5.3 %copy.81 = f32[32,4,4096]{2,0,1:T(8,128)S(1)} copy(f32[32,4,4096]{0,2,1:T(8,128)} %bitcast.124) | data formatting | bytes 4194304 | tf_op jit(solution)/shard_map/mul | solution.py:82
  136.4 2.7 convert_reduce_fusion
  139.1 3.9 fusion.41
  143.0 85.7 %all-reduce.5 = (f32[27,4,32]{2,0,1:T(8,128)S(1)}, f32[32]{0:T(128)}, f32[64]{0:T(128)}, f32[128]{0:T(128)}) all-reduce(f32[27,4,32]{2,0,1:T(8,128)S(1)} %fusion.41, f32[32]{0:T(128)S(1)} %get-tuple-element.159, f32[64]{0:T(128)S(1)} %get-tuple-element.157, ...), channel_id=1, replica_groups=mesh['sample'=32,'slab'=8] {'sample','slab'}, use_global_device_ids=true, to_apply=%region_3.4 | all-reduce | flops 3680 | bytes 29440 | tf_op jit(solution)/shard_map/psum | solution.py:186
  228.6 0.7 copy.86
  229.3 155.3 %all-reduce.9.cloned.1.call-done = (f32[27,32,64]{2,1,0:T(8,128)}, f32[27,64,128]{2,1,0:T(8,128)}) async-done(((f32[27,32,64]{2,1,0:T(8,128)}, f32[27,64,128]{2,1,0:T(8,128)}), (f32[27,32,64]{2,1,0:T(8,128)}, f32[27,64,128]{2,1,0:T(8,128)})) %all-reduce.9.cloned.1.call-update) | async-done | bytes 1105936 | tf_op jit(solution)/shard_map/psum | solution.py:186
  384.6 1.8 copy.184
  386.4 2.2 copy.185
  (136 shorter events, 10.9 us)
Async XLA Ops:
  7.2 377.4 %all-reduce.9.cloned.1.call-start = ((), (), s32[]{:S(2)}) async-start(), calls=%async_computation | async-start | bytes 2654208 | tf_op jit(solution)/shard_map/psum | solution.py:186
  8.3 9.7 %collective-permute-start = (bf16[4,1,1,4096]{3,0,2,1:T(4,128)(2,1)S(1)}, bf16[4,1,1,4096]{3,0,2,1:T(4,128)(2,1)S(1)}, u32[]{:S(2)}, u32[]{:S(2)}) collective-permute-start(bf16[4,1,1,4096]{3,0,2,1:T(4,128)(2,1)S(1)} %get-tuple-element.223), channel_id=1, source_target_pairs={{0,1},{1,2},{2,3},{3,4},{4,5},{5,6},{6,7},{8,9},{9,10},{10,11},{11... | collective-permute-start | bytes 98312 | tf_op jit(solution)/shard_map/ppermute | solution.py:17
  12.6 5.3 %collective-permute-start.1 = (bf16[4,1,1,4096]{3,0,2,1:T(4,128)(2,1)S(1)}, bf16[4,1,1,4096]{3,0,2,1:T(4,128)(2,1)S(1)}, u32[]{:S(2)}, u32[]{:S(2)}) collective-permute-start(bf16[4,1,1,4096]{3,0,2,1:T(4,128)(2,1)S(1)} %get-tuple-element.224), channel_id=1, source_target_pairs={{1,0},{2,1},{3,2},{4,3},{5,4},{6,5},{7,6},{9,8},{10,9},{11,10},{12... | collective-permute-start | bytes 98312 | tf_op jit(solution)/shard_map/ppermute | solution.py:18
  18.0 2.7 copy-start.8
  18.0 0.6 copy-start.3
  18.6 0.6 copy-start.5
  19.4 1.3 copy-start.4
  19.4 1.3 copy-start.6
  57.7 6.0 %collective-permute-start.2 = (bf16[32,1,1,1024]{3,0,2,1:T(8,128)(2,1)S(1)}, bf16[32,1,1,1024]{3,0,2,1:T(8,128)(2,1)S(1)}, u32[]{:S(2)}, u32[]{:S(2)}) collective-permute-start(bf16[32,1,1,1024]{3,0,2,1:T(8,128)(2,1)S(1)} %get-tuple-element.219), channel_id=1, source_target_pairs={{0,1},{1,2},{2,3},{3,4},{4,5},{5,6},{6,7},{8,9},{9,10},{10,11},{11... | collective-permute-start | bytes 196616 | tf_op jit(solution)/shard_map/ppermute | solution.py:17
  61.9 5.2 %collective-permute-start.3 = (bf16[32,1,1,1024]{3,0,2,1:T(8,128)(2,1)S(1)}, bf16[32,1,1,1024]{3,0,2,1:T(8,128)(2,1)S(1)}, u32[]{:S(2)}, u32[]{:S(2)}) collective-permute-start(bf16[32,1,1,1024]{3,0,2,1:T(8,128)(2,1)S(1)} %get-tuple-element.220), channel_id=1, source_target_pairs={{1,0},{2,1},{3,2},{4,3},{5,4},{6,5},{7,6},{9,8},{10,9},{11,10},{12... | collective-permute-start | bytes 196616 | tf_op jit(solution)/shard_map/ppermute | solution.py:18
  67.3 4.2 %copy-start.2 = (bf16[27,32,64]{2,1,0:T(8,128)(2,1)S(1)}, bf16[27,32,64]{2,1,0:T(8,128)(2,1)}, u32[]{:S(2)}) copy-start(bf16[27,32,64]{2,1,0:T(8,128)(2,1)} %param.12) | copy-start | bytes 331780
  67.3 4.2 %copy-start.9 = (f32[64]{0:T(128)S(1)}, f32[64]{0:T(128)}, u32[]{:S(2)}) copy-start(f32[64]{0:T(128)} %param.13) | copy-start | bytes 772
  69.8 1.7 copy-start
  71.5 8.3 %copy-start.7 = (bf16[128,1,1,256]{3,0,2,1:T(8,128)(2,1)S(1)}, bf16[128,1,1,256]{3,0,2,1:T(8,128)(2,1)}, u32[]{:S(2)}) copy-start(bf16[128,1,1,256]{3,0,2,1:T(8,128)(2,1)} %param.9) | copy-start | bytes 196612
  73.1 14.4 %collective-permute-start.5 = (bf16[64,1,1,256]{0,3,2,1:T(8,128)(2,1)S(1)}, bf16[64,1,1,256]{0,3,2,1:T(8,128)(2,1)S(1)}, u32[]{:S(2)}, u32[]{:S(2)}) collective-permute-start(bf16[64,1,1,256]{0,3,2,1:T(8,128)(2,1)S(1)} %fusion.106), channel_id=1, source_target_pairs={{1,0},{2,1},{3,2},{4,3},{5,4},{6,5},{7,6},{9,8},{10,9},{11,10},{12... | collective-permute-start | bytes 98312 | tf_op jit(solution)/shard_map/ppermute | solution.py:18
  74.4 13.1 %collective-permute-start.4 = (bf16[64,1,1,256]{0,3,2,1:T(8,128)(2,1)S(1)}, bf16[64,1,1,256]{0,3,2,1:T(8,128)(2,1)S(1)}, u32[]{:S(2)}, u32[]{:S(2)}) collective-permute-start(bf16[64,1,1,256]{0,3,2,1:T(8,128)(2,1)S(1)} %fusion.106), channel_id=1, source_target_pairs={{0,1},{1,2},{2,3},{3,4},{4,5},{5,6},{6,7},{8,9},{9,10},{10,11},{11... | collective-permute-start | bytes 98312 | tf_op jit(solution)/shard_map/ppermute | solution.py:17
  87.6 4.9 %copy-start.10 = (f32[128]{0:T(128)S(1)}, f32[128]{0:T(128)}, u32[]{:S(2)}) copy-start(f32[128]{0:T(128)} %param.15) | copy-start | bytes 1540
  93.9 8.6 %collective-permute-start.7 = (bf16[128,1,1,256]{0,3,2,1:T(8,128)(2,1)S(1)}, bf16[128,1,1,256]{0,3,2,1:T(8,128)(2,1)S(1)}, u32[]{:S(2)}, u32[]{:S(2)}) collective-permute-start(bf16[128,1,1,256]{0,3,2,1:T(8,128)(2,1)S(1)} %get-tuple-element.156), channel_id=1, source_target_pairs={{1,0},{2,1},{3,2},{4,3},{5,4},{6,5},{7,6},{9,8},{10,9},{11,10},{12... | collective-permute-start | bytes 196616 | tf_op jit(solution)/shard_map/ppermute | solution.py:18
  95.2 7.3 %collective-permute-start.6 = (bf16[128,1,1,256]{0,3,2,1:T(8,128)(2,1)S(1)}, bf16[128,1,1,256]{0,3,2,1:T(8,128)(2,1)S(1)}, u32[]{:S(2)}, u32[]{:S(2)}) collective-permute-start(bf16[128,1,1,256]{0,3,2,1:T(8,128)(2,1)S(1)} %get-tuple-element.156), channel_id=1, source_target_pairs={{0,1},{1,2},{2,3},{3,4},{4,5},{5,6},{6,7},{8,9},{9,10},{10,11},{11... | collective-permute-start | bytes 196616 | tf_op jit(solution)/shard_map/ppermute | solution.py:17
  106.6 9.9 %collective-permute-start.8 = (bf16[64,1,1,1024]{3,0,2,1:T(8,128)(2,1)S(1)}, bf16[64,1,1,1024]{3,0,2,1:T(8,128)(2,1)S(1)}, u32[]{:S(2)}, u32[]{:S(2)}) collective-permute-start(bf16[64,1,1,1024]{3,0,2,1:T(8,128)(2,1)S(1)} %get-tuple-element.165), channel_id=1, source_target_pairs={{0,1},{1,2},{2,3},{3,4},{4,5},{5,6},{6,7},{8,9},{9,10},{10,11},{11... | collective-permute-start | bytes 393224 | tf_op jit(solution)/shard_map/ppermute | solution.py:17
  111.1 6.9 %collective-permute-start.9 = (bf16[64,1,1,1024]{3,0,2,1:T(8,128)(2,1)S(1)}, bf16[64,1,1,1024]{3,0,2,1:T(8,128)(2,1)S(1)}, u32[]{:S(2)}, u32[]{:S(2)}) collective-permute-start(bf16[64,1,1,1024]{3,0,2,1:T(8,128)(2,1)S(1)} %get-tuple-element.166), channel_id=1, source_target_pairs={{1,0},{2,1},{3,2},{4,3},{5,4},{6,5},{7,6},{9,8},{10,9},{11,10},{12... | collective-permute-start | bytes 393224 | tf_op jit(solution)/shard_map/ppermute | solution.py:18
  136.3 2.7 copy-start.1
Sparse Core Ops, SparseCore 0:
  116.6 267.9 all-reduce.8
where the time goes:
time: 400 us; the launch traced here: 396 us
  waiting for transfers between devices  160 us (40%)
  blocking collectives  85.7 us (21%)
  local copies, waits for them, and re-layouts  61 us (15%)
  starting transfers between devices  30.9 us (8%)
  other arithmetic  24.5 us (6%)
  matrix products  18 us (4%)
  between operations  15.3 us (4%)
    psum x1, waiting for transfers between devices, per_device(): lax.psum((kernel_first, bias_first, kernel_second, bias_second), ('sample...  155 us
    psum x1, blocking collectives, per_device(): lax.psum((kernel_first, bias_first, kernel_second, bias_second), ('sample...  85.7 us
    ppermute x5, starting transfers between devices, with_halo(): before = lax.ppermute(last, axis, up)  23.7 us
    concatenate x3, local copies, waits for them, and re-layouts, gather_taps(): return jnp.concatenate(pieces, axis=0)  20.2 us
    unnamed x52, local copies, waits for them, and re-layouts  12.9 us
    reduce_sum x2, other arithmetic, pool_cells(): grouped.mean(axis=(3, 5, 7))  9.96 us
    dot_general x3, matrix products, weight_term(): jnp.einsum('kgzp,ogzp->ko', patches, grad_block, preferred_element_type=j...  9.02 us
    dot_general x5, matrix products, apply_weight(): jnp.einsum('ko,kgzp->ogzp', flat_weight, patches, preferred_element_type=...  8.99 us
  transfers between devices with their start and end apart: 11, of which 3 were waited for; matrix products, arithmetic and copies ran while one was open for 11% of the time, Pallas kernels for 0%

commit v1 on v0

--- a/solution.py
+++ b/solution.py
@@ -184,7 +184,7 @@
     kernel_first = weight_grads(volume_padded, first_delta, SX, CZ, w_first)
     bias_first = bias_sum(first_delta)
     kernel_first, bias_first, kernel_second, bias_second = lax.psum(
-        (kernel_first, bias_first, kernel_second, bias_second), ("sample", "slab")
+        lax.psum((kernel_first, bias_first, kernel_second, bias_second), "sample"), "slab"
     )
     return (
         features,

time: 400 us -> 581 us (1.45)
  blocking collectives: 85.7 us -> 220 us
  waiting for transfers between devices: 160 us -> 207 us
    psum x1 -> x3, blocking collectives: 85.7 us -> 220 us  [the longest x1 120 us: per_device(): lax.psum((kernel_first, bias_first, kernel_second, bias_second), 'sample')]
    psum x1 -> x3, waiting for transfers between devices: 155 us -> 204 us  [the longest x1 117 us: per_device(): lax.psum((kernel_first, bias_first, kernel_second, bias_second), 'sample')]
  transfers between devices with their start and end apart: 11 -> 13, of which waited for: 3 -> 3; matrix products, arithmetic and copies ran while one was open for 11% -> 7% of each run, Pallas kernels for 0% -> 0%
where the time goes in v1:
time: 581 us; the launch traced here: 577 us
  blocking collectives  220 us (38%)
  waiting for transfers between devices  207 us (36%)
  local copies, waits for them, and re-layouts  61.2 us (11%)
  starting transfers between devices  30.8 us (5%)
  other arithmetic  24.5 us (4%)
  matrix products  18 us (3%)
  between operations  15 us (3%)
    psum x1, blocking collectives, per_device(): lax.psum((kernel_first, bias_first, kernel_second, bias_second), 'sample')  120 us
    psum x1, waiting for transfers between devices, per_device(): lax.psum((kernel_first, bias_first, kernel_second, bias_second), 'sample')  117 us
    psum x1, waiting for transfers between devices, per_device(): lax.psum((kernel_third, bias_third), ('sample', 'slab'))  86.8 us
    psum x1, blocking collectives, per_device(): lax.psum((kernel_third, bias_third), ('sample', 'slab'))  77.1 us
    ppermute x5, starting transfers between devices, with_halo(): before = lax.ppermute(last, axis, up)  23.7 us
    psum x1, blocking collectives, per_device(): lax.psum(lax.psum((kernel_first, bias_first, kernel_second, bias_second),...  23 us
    concatenate x3, local copies, waits for them, and re-layouts, gather_taps(): return jnp.concatenate(pieces, axis=0)  20.3 us
    unnamed x52, local copies, waits for them, and re-layouts  12.9 us
  transfers between devices with their start and end apart: 13, of which 3 were waited for; matrix products, arithmetic and copies ran while one was open for 7% of the time, Pallas kernels for 0%

profile of v1, /device:TPU:1, one launch (start us, length us, event | category | flops | bytes accessed | tf_op | source)
XLA Modules:
  0.0 576.9 jit_solution(14404217917900565659)
XLA Ops:
  7.2 1.0 copy.58
  8.3 4.4 collective-permute-start
  12.6 1.3 collective-permute-start.1
  14.6 0.9 reverse_bitcast_fusion.1
  15.5 1.0 reverse_bitcast_fusion
  16.6 1.4 reshape.324
  18.0 0.6 copy-done.3
  18.6 0.6 copy-done.5
  19.4 1.3 slice_multiply_fusion.36
  20.7 1.7 slice_multiply_fusion.37
  22.4 16.3 %concatenate.62 = bf16[108,1,4,4096]{3,0,2,1:T(8,128)(2,1)} concatenate(bf16[4,1,4,4096]{3,0,2,1:T(4,128)(2,1)} %get-tuple-element.212, bf16[4,1,4,4096]{3,0,2,1:T(4,128)(2,1)S(1)} %get-tuple-element.218, bf16[4,1,4,4096]{3,0,2,1:T(4,128)(2,1)S(1)} %get-tuple-element.203, bf16[4,1,4,4096]{3,0,2,1:T(4,128)(2,1)} %get-tuple-element.211, ...), dimensions={0} | concatenate | bytes 7077888 | tf_op jit(solution)/shard_map/while/body/eval_jaxpr/concatenate | solution.py:53
  38.7 4.7 fusion.10
  43.3 4.7 copy.65
  48.0 9.5 %reduce_sum.54 = f32[32,2,64,16]{0,3,2,1:T(8,128)S(1)} reduce(f32[32,2,2,64,2,16,2]{0,6,5,4,3,2,1:T(2,128)} %bitcast.123, f32[]{:T(128)} %constant.224.clone.1), dimensions={2,4,6}, to_apply=%region_0.1 | reduce | flops 458752 | bytes 2359300 | tf_op jit(solution)/shard_map/while/body/eval_jaxpr/reduce_sum | solution.py:72
  57.8 4.2 collective-permute-start.2
  62.0 1.8 collective-permute-start.3
  63.9 3.3 collective-permute-done.3
  69.9 1.7 copy-done
  71.7 0.9 multiply_reduce_fusion
  73.2 1.3 collective-permute-start.5
  74.5 5.4 collective-permute-start.4
  79.9 0.7 copy.75
  81.0 6.6 %copy.74 = bf16[108,4096,4]{1,2,0:T(4,128)(2,1)} copy(bf16[108,4096,4]{1,0,2:T(8,128)(2,1)} %bitcast.125) | data formatting | bytes 7077888 | tf_op jit(solution)/shard_map/while/body/eval_jaxpr/kgzp,ogzp->ko/dot_general | solution.py:62
  87.8 0.8 slice_multiply_fusion.72
  88.6 3.4 concatenate.68
  92.0 0.6 copy.83
  92.7 1.4 convert_reduce_fusion.2
  94.1 1.3 collective-permute-start.7
  95.4 5.2 collective-permute-start.6
  100.6 1.3 fusion.107
  104.5 0.7 fusion.53
  105.9 3.8 convolution_bitcast_fusion
  109.9 4.6 collective-permute-start.8
  114.4 1.3 collective-permute-start.9
  115.7 117.2 %all-reduce.11.cloned.1.call-done = f32[27,32,64]{2,1,0:T(8,128)} async-done(((f32[27,32,64]{2,1,0:T(8,128)}), f32[27,32,64]{2,1,0:T(8,128)}) %all-reduce.11.cloned.1.call-update) | async-done | bytes 221200 | tf_op jit(solution)/shard_map/psum | solution.py:187
  233.0 0.7 copy.85
  233.8 77.1 %psum.79 = f32[128]{0:T(128)} all-reduce(f32[128]{0:T(128)S(1)} %get-tuple-element.150), channel_id=1, replica_groups=mesh['sample'=32,'slab'=8] {'sample','slab'}, use_global_device_ids=true, to_apply=%region_15.16 | all-reduce | flops 128 | bytes 1024 | tf_op jit(solution)/shard_map/psum | solution.py:169
  314.7 1.3 fusion.35
  316.4 7.6 %broadcast_in_dim.14 = f32[32,2,2,64,2,16,2]{0,6,5,4,3,2,1:T(2,128)} broadcast(f32[32,2,64,16]{0,3,2,1:T(8,128)S(1)} %bitcast.130), dimensions={0,1,3,5} | broadcast | bytes 2359296 | tf_op jit(solution)/shard_map/broadcast_in_dim | solution.py:79
  323.9 5.3 copy.81
  329.3 2.7 convert_reduce_fusion
  332.0 3.9 fusion.41
  335.9 119.9 %all-reduce.5 = (f32[27,4,32]{2,0,1:T(8,128)S(1)}, f32[32]{0:T(128)S(1)}, f32[64]{0:T(128)S(1)}) all-reduce(f32[27,4,32]{2,0,1:T(8,128)S(1)} %fusion.41, f32[32]{0:T(128)S(1)} %get-tuple-element.159, f32[64]{0:T(128)S(1)} %get-tuple-element.157), channel_id=1, replica_groups=mesh['sample'=32,'slab'=8] {'sample'}, use_global_device_ids=true, to_apply=%region_3.4 | all-reduce | flops 3552 | bytes 28416 | tf_op jit(solution)/shard_map/psum | solution.py:187
  455.8 23.0 %all-reduce.6 = (f32[27,4,32]{2,0,1:T(8,128)S(1)}, f32[32]{0:T(128)}, f32[64]{0:T(128)}) all-reduce(f32[27,4,32]{2,0,1:T(8,128)S(1)} %get-tuple-element.139, f32[32]{0:T(128)S(1)} %get-tuple-element.140, f32[64]{0:T(128)S(1)} %get-tuple-element.146), channel_id=1, replica_groups=mesh['sample'=32,'slab'=8] {'slab'}, use_global_device_ids=true, to_apply=%region_4.5 | all-reduce | flops 3552 | bytes 28416 | tf_op jit(solution)/shard_map/psum | solution.py:186
  478.8 0.7 copy.86
  479.5 86.8 %all-reduce.15.cloned.1.call-done = f32[27,64,128]{2,1,0:T(8,128)} async-done(((f32[27,64,128]{2,1,0:T(8,128)}), f32[27,64,128]{2,1,0:T(8,128)}) %all-reduce.15.cloned.1.call-update) | async-done | bytes 884752 | tf_op jit(solution)/shard_map/psum | solution.py:169
  566.2 1.8 copy.185
  568.0 2.2 copy.186
  (144 shorter events, 12.1 us)
Async XLA Ops:
  7.2 225.7 %all-reduce.11.cloned.1.call-start = ((), (), s32[]{:S(2)}) async-start(), calls=%async_computation | async-start | bytes 884736 | tf_op jit(solution)/shard_map/psum | solution.py:187
  8.3 9.7 %collective-permute-start = (bf16[4,1,1,4096]{3,0,2,1:T(4,128)(2,1)S(1)}, bf16[4,1,1,4096]{3,0,2,1:T(4,128)(2,1)S(1)}, u32[]{:S(2)}, u32[]{:S(2)}) collective-permute-start(bf16[4,1,1,4096]{3,0,2,1:T(4,128)(2,1)S(1)} %get-tuple-element.223), channel_id=1, source_target_pairs={{0,1},{1,2},{2,3},{3,4},{4,5},{5,6},{6,7},{8,9},{9,10},{10,11},{11... | collective-permute-start | bytes 98312 | tf_op jit(solution)/shard_map/ppermute | solution.py:17
  12.6 5.3 collective-permute-start.1
  18.0 2.7 copy-start.8
  18.0 0.6 copy-start.3
  18.6 0.6 copy-start.5
  19.4 1.3 copy-start.4
  19.4 1.3 copy-start.6
  57.8 6.0 %collective-permute-start.2 = (bf16[32,1,1,1024]{3,0,2,1:T(8,128)(2,1)S(1)}, bf16[32,1,1,1024]{3,0,2,1:T(8,128)(2,1)S(1)}, u32[]{:S(2)}, u32[]{:S(2)}) collective-permute-start(bf16[32,1,1,1024]{3,0,2,1:T(8,128)(2,1)S(1)} %get-tuple-element.219), channel_id=1, source_target_pairs={{0,1},{1,2},{2,3},{3,4},{4,5},{5,6},{6,7},{8,9},{9,10},{10,11},{11... | collective-permute-start | bytes 196616 | tf_op jit(solution)/shard_map/ppermute | solution.py:17
  62.0 5.2 collective-permute-start.3
  67.4 4.3 copy-start.2
  67.4 4.2 copy-start.9
  69.9 1.8 copy-start
  71.7 8.2 %copy-start.7 = (bf16[128,1,1,256]{3,0,2,1:T(8,128)(2,1)S(1)}, bf16[128,1,1,256]{3,0,2,1:T(8,128)(2,1)}, u32[]{:S(2)}) copy-start(bf16[128,1,1,256]{3,0,2,1:T(8,128)(2,1)} %param.9) | copy-start | bytes 196612
  73.2 14.4 %collective-permute-start.5 = (bf16[64,1,1,256]{0,3,2,1:T(8,128)(2,1)S(1)}, bf16[64,1,1,256]{0,3,2,1:T(8,128)(2,1)S(1)}, u32[]{:S(2)}, u32[]{:S(2)}) collective-permute-start(bf16[64,1,1,256]{0,3,2,1:T(8,128)(2,1)S(1)} %fusion.106), channel_id=1, source_target_pairs={{1,0},{2,1},{3,2},{4,3},{5,4},{6,5},{7,6},{9,8},{10,9},{11,10},{12... | collective-permute-start | bytes 98312 | tf_op jit(solution)/shard_map/ppermute | solution.py:18
  74.5 13.1 %collective-permute-start.4 = (bf16[64,1,1,256]{0,3,2,1:T(8,128)(2,1)S(1)}, bf16[64,1,1,256]{0,3,2,1:T(8,128)(2,1)S(1)}, u32[]{:S(2)}, u32[]{:S(2)}) collective-permute-start(bf16[64,1,1,256]{0,3,2,1:T(8,128)(2,1)S(1)} %fusion.106), channel_id=1, source_target_pairs={{0,1},{1,2},{2,3},{3,4},{4,5},{5,6},{6,7},{8,9},{9,10},{10,11},{11... | collective-permute-start | bytes 98312 | tf_op jit(solution)/shard_map/ppermute | solution.py:17
  87.8 4.9 copy-start.10
  94.1 7.8 %collective-permute-start.7 = (bf16[128,1,1,256]{0,3,2,1:T(8,128)(2,1)S(1)}, bf16[128,1,1,256]{0,3,2,1:T(8,128)(2,1)S(1)}, u32[]{:S(2)}, u32[]{:S(2)}) collective-permute-start(bf16[128,1,1,256]{0,3,2,1:T(8,128)(2,1)S(1)} %get-tuple-element.156), channel_id=1, source_target_pairs={{1,0},{2,1},{3,2},{4,3},{5,4},{6,5},{7,6},{9,8},{10,9},{11,10},{12... | collective-permute-start | bytes 196616 | tf_op jit(solution)/shard_map/ppermute | solution.py:18
  95.4 6.5 %collective-permute-start.6 = (bf16[128,1,1,256]{0,3,2,1:T(8,128)(2,1)S(1)}, bf16[128,1,1,256]{0,3,2,1:T(8,128)(2,1)S(1)}, u32[]{:S(2)}, u32[]{:S(2)}) collective-permute-start(bf16[128,1,1,256]{0,3,2,1:T(8,128)(2,1)S(1)} %get-tuple-element.156), channel_id=1, source_target_pairs={{0,1},{1,2},{2,3},{3,4},{4,5},{5,6},{6,7},{8,9},{9,10},{10,11},{11... | collective-permute-start | bytes 196616 | tf_op jit(solution)/shard_map/ppermute | solution.py:17
  109.8 369.7 %all-reduce.13.cloned.1.call-start = ((), (), s32[]{:S(2)}) async-start(), calls=%async_computation.1 | async-start | bytes 884736 | tf_op jit(solution)/shard_map/psum | solution.py:186
  109.9 201.1 %collective-permute-start.8 = (bf16[64,1,1,1024]{3,0,2,1:T(8,128)(2,1)S(1)}, bf16[64,1,1,1024]{3,0,2,1:T(8,128)(2,1)S(1)}, u32[]{:S(2)}, u32[]{:S(2)}) collective-permute-start(bf16[64,1,1,1024]{3,0,2,1:T(8,128)(2,1)S(1)} %get-tuple-element.165), channel_id=1, source_target_pairs={{0,1},{1,2},{2,3},{3,4},{4,5},{5,6},{6,7},{8,9},{9,10},{10,11},{11... | collective-permute-start | bytes 393224 | tf_op jit(solution)/shard_map/ppermute | solution.py:17
  114.4 196.5 %collective-permute-start.9 = (bf16[64,1,1,1024]{3,0,2,1:T(8,128)(2,1)S(1)}, bf16[64,1,1,1024]{3,0,2,1:T(8,128)(2,1)S(1)}, u32[]{:S(2)}, u32[]{:S(2)}) collective-permute-start(bf16[64,1,1,1024]{3,0,2,1:T(8,128)(2,1)S(1)} %get-tuple-element.166), channel_id=1, source_target_pairs={{1,0},{2,1},{3,2},{4,3},{5,4},{6,5},{7,6},{9,8},{10,9},{11,10},{12... | collective-permute-start | bytes 393224 | tf_op jit(solution)/shard_map/ppermute | solution.py:18
  232.9 333.3 %all-reduce.15.cloned.1.call-start = ((), (), s32[]{:S(2)}) async-start(), calls=%async_computation.2 | async-start | bytes 1769472 | tf_op jit(solution)/shard_map/psum | solution.py:169
  329.3 2.7 copy-start.1
Sparse Core Ops, SparseCore 0:
  109.9 122.9 all-reduce.10
  235.4 67.7 all-reduce.12
  309.2 256.9 all-reduce.14
